TPU v7x, 32 devices: a whole 2x2x4 slice. The times are simulated.
32 devices in a mesh: group: 2 (over y), head: 4 (over x, core), seq: 4 (over z).
Axes of the slice: x: 2, y: 2, z: 4, core: 2. Of those that a mesh axis runs over, the one named last changes fastest.
Arguments:
- new_queries: bfloat16 [512, 4096], P(('group', 'seq'), 'head'), parts along dimension 0, may hold values from -80 to 80
- new_keys: bfloat16 [512, 1024], P(('group', 'seq'), 'head'), parts along dimension 0, may hold values from -6 to 6
- new_values: bfloat16 [512, 1024], P(('group', 'seq'), 'head'), parts along dimension 0, may hold values from -6 to 6
- cache_keys: bfloat16 [8192, 1024], P(('group', 'seq'), 'head'), parts along dimension 0, may hold values from -5 to 5
- cache_values: bfloat16 [8192, 1024], P(('group', 'seq'), 'head'), parts along dimension 0, may hold values from -6 to 6
- segment_ids: int32 [512], P('group'), parts along dimension 0, may hold values from 0 to 7, as said below
- cache_length: int32 [2], P('group'), parts along dimension 0, may hold values from 512 to 4096
Outputs:
- attended: bfloat16 [512, 4096], P(('group', 'seq'), 'head'), parts along dimension 0
There are 2 independent parts, one for each index of `group`. A program takes and returns all parts, laid end to end along the dimension named above; each array names one. Nothing has to cross between parts.
Inputs may be any that keep to these rules, and one draw needn't show every extreme that they name: `segment_ids`: Non-decreasing along the positions; every number of 0 to 7 appears.
All inputs are finite; a program needn't handle non-finite values.
Results may differ from a plain program's by a relative error of at most 0.0024.
Values may be sent and summed in bfloat16 or wider, within the bound.
No kernel may reach another device: no remote copies, remote signals or barrier semaphores. Data moves between devices by JAX's collectives and lax.ppermute only.
A program may use at most 64 MiB of HBM per device.

v0:
```python
import jax
import jax.numpy as jnp
from jax import lax
from jax.sharding import PartitionSpec as P

HEAD_DIM = 128
NEG_FILL = -1e30


def on_device(
    new_queries, new_keys, new_values, cache_keys, cache_values, segment_ids, cache_length
):
    head_size = HEAD_DIM
    own_count = new_queries.shape[0]
    join_rows = segment_ids.shape[0]
    cache_rows = cache_keys.shape[0]
    heads_kv = cache_keys.shape[1] // head_size
    heads_q = new_queries.shape[1] // head_size
    group_size = heads_q // heads_kv
    seq_count = lax.axis_size("seq")
    seq_rank = lax.axis_index("seq")
    score_scale = head_size ** (-0.5)
    cache_limit = cache_length[0]
    all_queries, all_keys, all_values = (
        lax.all_gather(new_queries, "seq", axis=0, tiled=True),
        lax.all_gather(new_keys, "seq", axis=0, tiled=True),
        lax.all_gather(new_values, "seq", axis=0, tiled=True),
    )
    keys_here, values_here = (cache_keys, cache_values)
    live_rows = jnp.clip(cache_limit - seq_rank * cache_rows, 0, cache_rows)
    tile_width = min(cache_rows // seq_count, 256)
    block_rows = min(256, cache_rows)
    tiles_per_block = block_rows // tile_width
    block_total = (live_rows + block_rows - 1) // block_rows
    keys_tiled = keys_here.reshape(cache_rows, heads_kv, head_size)
    values_tiled = values_here.reshape(cache_rows, heads_kv, head_size)
    query_block = min(64, join_rows)
    grouped = all_queries.reshape(
        join_rows // query_block, query_block, heads_kv, group_size, head_size
    )

    def one_block(block_queries):

        def step_pass(block_index, running):
            best, numer_acc, denom_acc = running
            start = block_index * block_rows
            key_tile = lax.dynamic_slice_in_dim(keys_tiled, start, block_rows, 0)
            scores = (
                jnp.einsum(
                    "cgrd,tgd->cgrt", block_queries, key_tile, preferred_element_type=jnp.float32
                )
                * score_scale
            )
            usable = (start + jnp.arange(block_rows, dtype=jnp.int32) < live_rows).reshape(
                tiles_per_block, tile_width
            )
            split = scores.reshape(query_block, heads_kv, group_size, tiles_per_block, tile_width)
            tile_max = jnp.max(jnp.where(usable, split, NEG_FILL), axis=-1)
            weights = jnp.exp(jnp.where(usable, split - tile_max[..., None], NEG_FILL)).astype(
                jnp.bfloat16
            )
            value_tile = lax.dynamic_slice_in_dim(values_tiled, start, block_rows, 0).reshape(
                tiles_per_block, tile_width, heads_kv, head_size
            )
            tile_numer = jnp.einsum(
                "cgrbt,btgd->cgrbd", weights, value_tile, preferred_element_type=jnp.float32
            )
            tile_denom = jnp.sum(weights.astype(jnp.float32), axis=-1)
            new_best = jnp.maximum(best, jnp.max(tile_max, axis=-1))
            keep = jnp.exp(best - new_best)
            factor = jnp.exp(tile_max - new_best[..., None])
            numer_acc = numer_acc * keep[..., None] + jnp.sum(
                tile_numer * factor[..., None], axis=3
            )
            denom_acc = denom_acc * keep + jnp.sum(tile_denom * factor, axis=-1)
            return (new_best, numer_acc, denom_acc)

        start_state = (
            jnp.full((query_block, heads_kv, group_size), NEG_FILL, jnp.float32),
            jnp.zeros((query_block, heads_kv, group_size, head_size), jnp.float32),
            jnp.zeros((query_block, heads_kv, group_size), jnp.float32),
        )
        return lax.fori_loop(0, block_total, step_pass, start_state)

    block_best, block_numer, block_denom = lax.map(one_block, grouped)
    cache_max = block_best.reshape(join_rows, heads_kv, group_size)
    cache_numer = block_numer.reshape(join_rows, heads_kv, group_size, head_size)
    cache_denom = block_denom.reshape(join_rows, heads_kv, group_size)
    own_queries = new_queries.reshape(own_count, heads_kv, group_size, head_size)
    fresh_scores = (
        jnp.einsum(
            "cgrd,tgd->cgrt",
            own_queries,
            all_keys.reshape(join_rows, heads_kv, head_size),
            preferred_element_type=jnp.float32,
        )
        * score_scale
    )
    start_row = seq_rank * own_count
    own_positions = start_row + jnp.arange(own_count, dtype=jnp.int32)
    own_segments = lax.dynamic_slice_in_dim(segment_ids, start_row, own_count, 0)
    key_positions = jnp.arange(join_rows, dtype=jnp.int32)
    allowed = (key_positions[None, :] <= own_positions[:, None]) & (
        segment_ids[None, :] == own_segments[:, None]
    )
    allowed = allowed[:, None, None, :]
    fresh_max = jnp.max(jnp.where(allowed, fresh_scores, NEG_FILL), axis=-1)
    zero_index = jnp.zeros((), jnp.int32)
    merged = lax.dynamic_update_slice(
        cache_max,
        jnp.maximum(lax.dynamic_slice_in_dim(cache_max, start_row, own_count, 0), fresh_max),
        (start_row, zero_index, zero_index),
    )
    row_max = (
        lax.pmax(merged.reshape(join_rows, heads_q).astype(jnp.bfloat16), "seq")
        .astype(jnp.float32)
        .reshape(join_rows, heads_kv, group_size)
    )
    rescale = jnp.exp(cache_max - row_max)
    scaled_numer = (cache_numer * rescale[..., None]).reshape(join_rows, heads_q * head_size)
    scaled_denom = (cache_denom * rescale).reshape(join_rows, heads_q)
    own_numer, own_denom = (
        lax.psum_scatter(scaled_numer, "seq", scatter_dimension=0, tiled=True),
        lax.psum_scatter(scaled_denom, "seq", scatter_dimension=0, tiled=True),
    )
    own_max = lax.dynamic_slice_in_dim(row_max, start_row, own_count, 0)
    fresh_weights = jnp.exp(
        jnp.where(allowed, fresh_scores - fresh_max[..., None], NEG_FILL)
    ).astype(jnp.bfloat16)
    fresh_factor = jnp.exp(fresh_max - own_max)
    fresh_numer = (
        jnp.einsum(
            "cgrt,tgd->cgrd",
            fresh_weights,
            all_values.reshape(join_rows, heads_kv, head_size),
            preferred_element_type=jnp.float32,
        )
        * fresh_factor[..., None]
    )
    fresh_denom = jnp.sum(fresh_weights.astype(jnp.float32), axis=-1) * fresh_factor
    total_numer = own_numer + fresh_numer.reshape(own_count, heads_q * head_size)
    total_denom = own_denom + fresh_denom.reshape(own_count, heads_q)
    attended = total_numer.reshape(own_count, heads_q, head_size) / total_denom[..., None]
    return attended.reshape(own_count, heads_q * head_size).astype(jnp.bfloat16)


def solution(mesh):
    placed = (
        P(("group", "seq"), "head"),
        P(("group", "seq"), "head"),
        P(("group", "seq"), "head"),
        P(("group", "seq"), "head"),
        P(("group", "seq"), "head"),
        P("group"),
        P("group"),
    )
    return jax.shard_map(
        on_device,
        mesh=mesh,
        in_specs=placed,
        out_specs=P(("group", "seq"), "head"),
        check_vma=False,
    )
```

profile of v0, /device:TPU:0, one launch (start us, length us, event | category | flops | bytes accessed | tf_op | source)
XLA Modules:
  0.0 127.6 jit_solution(12809682222911493052)
XLA Ops:
  7.2 17.6 %all_gather.9 = bf16[256,1024]{1,0:T(8,128)(2,1)S(1)} all-gather(bf16[64,1024]{1,0:T(8,128)(2,1)} %param.11), channel_id=1, replica_groups=mesh['group'=2,'head'=4,'seq'=4] {'seq'}, dimensions={0}, use_global_device_ids=true | all-gather | bytes 655360 | tf_op jit(solution)/shard_map/all_gather | solution.py:25
  24.8 0.4 reshape.144
  25.2 0.7 copy-done.1
  26.3 1.3 copy.30
  27.9 18.3 %while.29 = (s32[]{:T(128)}, f32[4,64,2,4]{1,0,3,2:T(4,128)S(1)}, f32[4,64,2,4,128]{4,3,2,1,0:T(4,128)S(1)}, f32[4,64,2,4]{1,0,3,2:T(4,128)S(1)}, bf16[4,64,2,4,...) while((s32[]{:T(128)}, f32[4,64,2,4]{1,0,3,2:T(4,128)S(1)}, ...), condition=%wide.region_5.6_spmd, body=%wide.region_0.5_spmd.sunk | while | flops 68749824 | bytes 3850228 | solution.py:85
  28.0 4.1 %while.30 = (s32[]{:T(128)}, f32[64,2,4]{0,2,1:T(4,128)S(1)}, f32[64,2,4,128]{3,0,2,1:T(8,128)S(1)}, f32[64,2,4]{0,2,1:T(4,128)S(1)}, s32[]{:T(128)}, /*index=5*...) while((s32[]{:T(128)}, f32[64,2,4]{0,2,1:T(4,128)S(1)}, ...), condition=%wide.region_4.4_spmd, body=%wide.region_1.3_spmd.sunk | while | flops 68749824 | bytes 2526915 | solution.py:83
  32.6 4.1 %while.30 = (s32[]{:T(128)}, f32[64,2,4]{0,2,1:T(4,128)S(1)}, f32[64,2,4,128]{3,0,2,1:T(8,128)S(1)}, f32[64,2,4]{0,2,1:T(4,128)S(1)}, s32[]{:T(128)}, /*index=5*...) while((s32[]{:T(128)}, f32[64,2,4]{0,2,1:T(4,128)S(1)}, ...), condition=%wide.region_4.4_spmd, body=%wide.region_1.3_spmd.sunk | while | flops 68749824 | bytes 2526915 | solution.py:83
  37.1 4.1 %while.30 = (s32[]{:T(128)}, f32[64,2,4]{0,2,1:T(4,128)S(1)}, f32[64,2,4,128]{3,0,2,1:T(8,128)S(1)}, f32[64,2,4]{0,2,1:T(4,128)S(1)}, s32[]{:T(128)}, /*index=5*...) while((s32[]{:T(128)}, f32[64,2,4]{0,2,1:T(4,128)S(1)}, ...), condition=%wide.region_4.4_spmd, body=%wide.region_1.3_spmd.sunk | while | flops 68749824 | bytes 2526915 | solution.py:83
  41.7 4.1 %while.30 = (s32[]{:T(128)}, f32[64,2,4]{0,2,1:T(4,128)S(1)}, f32[64,2,4,128]{3,0,2,1:T(8,128)S(1)}, f32[64,2,4]{0,2,1:T(4,128)S(1)}, s32[]{:T(128)}, /*index=5*...) while((s32[]{:T(128)}, f32[64,2,4]{0,2,1:T(4,128)S(1)}, ...), condition=%wide.region_4.4_spmd, body=%wide.region_1.3_spmd.sunk | while | flops 68749824 | bytes 2526915 | solution.py:83
  46.5 0.7 copy-done.3
  47.1 13.3 %all_gather.10 = bf16[256,256]{1,0:T(8,128)(2,1)S(1)} all-gather(bf16[64,256]{1,0:T(8,128)(2,1)S(1)} %copy-done.3), channel_id=1, replica_groups=mesh['group'=2,'head'=4,'seq'=4] {'seq'}, dimensions={0}, use_global_device_ids=true | all-gather | bytes 163840 | tf_op jit(solution)/shard_map/all_gather | solution.py:26
  60.6 0.7 copy-done.5
  62.0 8.7 %pmax.7 = bf16[256,8]{0,1:T(8,128)(2,1)S(1)} all-reduce(bf16[256,8]{0,1:T(8,128)(2,1)S(1)} %convert_element_type.27), channel_id=1, replica_groups=mesh['group'=2,'head'=4,'seq'=4] {'seq'}, use_global_device_ids=true, to_apply=%region_7.8 | all-reduce | flops 2048 | bytes 8192 | tf_op jit(solution)/shard_map/pmax | solution.py:115
  70.7 0.8 copy.54
  71.6 0.4 reshape.147
  72.2 1.6 %mul.74 = f32[256,2,4,128]{3,2,1,0:T(4,128)} broadcast(f32[256,2,4]{2,1,0:T(2,128)S(1)} %copy.39), dimensions={0,1,2} | broadcast | bytes 1056768 | tf_op jit(solution)/shard_map/mul | solution.py:120
  73.8 1.6 %mul.75 = f32[256,1024]{1,0:T(8,128)S(1)} reshape(f32[256,2,4,128]{3,2,1,0:T(4,128)} %mul.74) | data formatting | bytes 2097152 | tf_op jit(solution)/shard_map/mul | solution.py:120
  75.4 1.2 mul.76
  76.6 0.7 copy-done.4
  77.3 13.5 %all_gather.11 = bf16[256,256]{1,0:T(8,128)(2,1)S(1)} all-gather(bf16[64,256]{1,0:T(8,128)(2,1)S(1)} %copy-done.4), channel_id=1, replica_groups=mesh['group'=2,'head'=4,'seq'=4] {'seq'}, dimensions={0}, use_global_device_ids=true | all-gather | bytes 163840 | tf_op jit(solution)/shard_map/all_gather | solution.py:27
  92.0 0.8 copy.55
  92.9 26.2 %reduce-scatter.5.cloned.1.call-done = f32[64,1024]{1,0:T(8,128)} async-done(((f32[256,1024]{1,0:T(8,128)}), f32[64,1024]{1,0:T(8,128)}) %reduce-scatter.5.cloned.1.call-update) | async-done | bytes 262160 | tf_op jit(solution)/shard_map/reduce_scatter | solution.py:123
  119.2 0.8 copy-done.2
  120.0 0.7 fusion.13
  (157 shorter events, 20.6 us)
Async XLA Ops:
  6.5 85.4 %reduce-scatter.7.cloned.1.call-start = ((), (), s32[]{:S(2)}) async-start(), calls=%async_computation.3 | async-start | bytes 163840
  24.8 1.0 copy-start.1
  27.9 18.4 %copy-start = (bf16[64,1024]{1,0:T(8,128)(2,1)S(1)}, bf16[64,1024]{1,0:T(8,128)(2,1)}, u32[]{:S(2)}) copy-start(bf16[64,1024]{1,0:T(8,128)(2,1)} %param.11) | copy-start | bytes 393220
  46.4 0.8 copy-start.3
  60.6 0.7 copy-start.5
  71.5 47.6 %reduce-scatter.5.cloned.1.call-start = ((), (), s32[]{:S(2)}) async-start(), calls=%async_computation.2 | async-start | bytes 1310720 | tf_op jit(solution)/shard_map/reduce_scatter | solution.py:123
  76.6 0.8 copy-start.4
  119.1 0.9 copy-start.2
Sparse Core Ops, SparseCore 0:
  71.6 19.7 reduce-scatter.6
  93.8 25.1 reduce-scatter.4
where the time goes:
time: 128 us
  blocking collectives  53.1 us (41%)
  waiting for transfers between devices  26.3 us (21%)
  between operations  14.3 us (11%)
  local copies, waits for them, and re-layouts  14.1 us (11%)
  matrix products  11.4 us (9%)
  other arithmetic  7.33 us (6%)
    reduce_scatter x1, waiting for transfers between devices, on_device(): lax.psum_scatter(scaled_numer, 'seq', scatter_dimension=0, tiled=True)  26.2 us
    all_gather x1, blocking collectives, on_device(): lax.all_gather(new_queries, 'seq', axis=0, tiled=True)  17.6 us
    all_gather x1, blocking collectives, on_device(): lax.all_gather(new_values, 'seq', axis=0, tiled=True)  13.5 us
    all_gather x1, blocking collectives, on_device(): lax.all_gather(new_keys, 'seq', axis=0, tiled=True)  13.3 us
    pmax x1, blocking collectives, on_device(): lax.pmax(merged.reshape(join_rows, heads_q).astype(jnp.bfloat16), 'seq')  8.67 us
    unnamed x17, local copies, waits for them, and re-layouts  6.63 us
    dot_general x16, matrix products, step_pass(): jnp.einsum('cgrbt,btgd->cgrbd', weights, value_tile, preferred_element_ty...  5.59 us
    dot_general x16, matrix products, step_pass(): jnp.einsum('cgrd,tgd->cgrt', block_queries, key_tile, preferred_element_t...  5.24 us
  transfers between devices with their start and end apart: 2, of which 1 were waited for; matrix products, arithmetic and copies ran while one was open for 5% of the time, Pallas kernels for 0%

commit v1 on v0

--- a/solution.py
+++ b/solution.py
@@ -1,3 +1,4 @@
+import functools
 import jax
 import jax.numpy as jnp
 from jax import lax
@@ -5,6 +6,24 @@
 
 HEAD_DIM = 128
 NEG_FILL = -1e30
+
+
+def carry_stocks(local, bus_axis):
+    mid_arr = jax.lax.axis_size(bus_axis)
+    shaped = jax.lax.axis_index(bus_axis)
+    vec_out, q_next, everything = (mid_arr, shaped, local.shape[0])
+    even, frame_out = (local, 1)
+    while frame_out < vec_out:
+        nodes = []
+        for t in tuple(range(vec_out)):
+            nodes.append((t, (t - frame_out) % vec_out))
+        even = jnp.concatenate([even, jax.lax.ppermute(even, bus_axis, nodes)], axis=0)
+        frame_out = 2 * frame_out
+    y = jnp.roll(even, q_next * everything, axis=0)
+    return y
+
+
+clusters_part = functools.partial(carry_stocks, bus_axis="seq")
 
 
 def on_device(
@@ -22,7 +41,7 @@
     score_scale = head_size ** (-0.5)
     cache_limit = cache_length[0]
     all_queries, all_keys, all_values = (
-        lax.all_gather(new_queries, "seq", axis=0, tiled=True),
+        clusters_part(new_queries),
         lax.all_gather(new_keys, "seq", axis=0, tiled=True),
         lax.all_gather(new_values, "seq", axis=0, tiled=True),
     )

time: 128 us -> 124 us (0.969)
  blocking collectives: 53.1 us -> 35.4 us
  starting transfers between devices: 0.04 us -> 5.81 us
  waiting for transfers between devices: 26.3 us -> 31 us
  local copies, waits for them, and re-layouts: 14.1 us -> 17.5 us
    all_gather x1 -> x0, blocking collectives: 17.6 us -> none  [on_device(): lax.all_gather(new_queries, 'seq', axis=0, tiled=True)]
    ppermute x0 -> x2, waiting for transfers between devices: none -> 6.66 us  [carry_stocks(): jax.lax.ppermute(even, bus_axis, nodes)]
    ppermute x0 -> x2, starting transfers between devices: none -> 5.76 us  [carry_stocks(): jax.lax.ppermute(even, bus_axis, nodes)]
    dynamic_update_slice x12, local copies, waits for them, and re-layouts: 1.12 us -> 3.81 us  [on_device(): block_best, block_numer, block_denom = lax.map(one_block, grouped)]
    reduce_scatter x1, waiting for transfers between devices: 26.2 us -> 24.3 us  [on_device(): lax.psum_scatter(scaled_numer, 'seq', scatter_dimension=0, tiled=True)]
    unnamed x17 -> x24, local copies, waits for them, and re-layouts: 6.63 us -> 5.08 us
  transfers between devices with their start and end apart: 2 -> 4, of which waited for: 1 -> 2; matrix products, arithmetic and copies ran while one was open for 5% -> 9% of each run, Pallas kernels for 0% -> 0%
where the time goes in v1:
time: 124 us
  blocking collectives  35.4 us (29%)
  waiting for transfers between devices  31 us (25%)
  local copies, waits for them, and re-layouts  17.5 us (14%)
  between operations  14.4 us (12%)
  matrix products  11.4 us (9%)
  other arithmetic  7.33 us (6%)
  starting transfers between devices  5.81 us (5%)
    reduce_scatter x1, waiting for transfers between devices, on_device(): lax.psum_scatter(scaled_numer, 'seq', scatter_dimension=0, tiled=True)  24.3 us
    all_gather x1, blocking collectives, on_device(): lax.all_gather(new_keys, 'seq', axis=0, tiled=True)  13.6 us
    all_gather x1, blocking collectives, on_device(): lax.all_gather(new_values, 'seq', axis=0, tiled=True)  13.5 us
    pmax x1, blocking collectives, on_device(): lax.pmax(merged.reshape(join_rows, heads_q).astype(jnp.bfloat16), 'seq')  8.38 us
    ppermute x2, waiting for transfers between devices, carry_stocks(): jax.lax.ppermute(even, bus_axis, nodes)  6.66 us
    ppermute x2, starting transfers between devices, carry_stocks(): jax.lax.ppermute(even, bus_axis, nodes)  5.76 us
    dot_general x16, matrix products, step_pass(): jnp.einsum('cgrbt,btgd->cgrbd', weights, value_tile, preferred_element_ty...  5.59 us
    dot_general x16, matrix products, step_pass(): jnp.einsum('cgrd,tgd->cgrt', block_queries, key_tile, preferred_element_t...  5.24 us
  transfers between devices with their start and end apart: 4, of which 2 were waited for; matrix products, arithmetic and copies ran while one was open for 9% of the time, Pallas kernels for 0%

profile of v1, /device:TPU:0, one launch (start us, length us, event | category | flops | bytes accessed | tf_op | source)
XLA Modules:
  0.0 123.9 jit_solution(9972568941000846922)
XLA Ops:
  6.5 5.0 %collective-permute-start = (bf16[64,1024]{1,0:T(8,128)(2,1)}, bf16[64,1024]{1,0:T(8,128)(2,1)S(1)}, u32[]{:S(2)}, u32[]{:S(2)}) collective-permute-start(bf16[64,1024]{1,0:T(8,128)(2,1)} %param.11), channel_id=1, source_target_pairs={{0,3},{1,0},{2,1},{3,2},{4,7},{5,4},{6,5},{7,6},{8,11},{9,8},{10,9... | collective-permute-start | bytes 393224 | tf_op jit(solution)/shard_map/ppermute | solution.py:20
  11.6 1.0 reshape.150
  12.6 13.6 %all_gather.6 = bf16[256,256]{1,0:T(8,128)(2,1)S(1)} all-gather(bf16[64,256]{1,0:T(8,128)(2,1)S(1)} %copy-done.4), channel_id=1, replica_groups=mesh['group'=2,'head'=4,'seq'=4] {'seq'}, dimensions={0}, use_global_device_ids=true | all-gather | bytes 163840 | tf_op jit(solution)/shard_map/all_gather | solution.py:45
  29.5 0.8 copy-done.2
  30.8 6.7 %collective-permute-done.1 = bf16[128,1024]{1,0:T(8,128)(2,1)S(1)} collective-permute-done((bf16[128,1024]{1,0:T(8,128)(2,1)S(1)}, bf16[128,1024]{1,0:T(8,128)(2,1)S(1)}, u32[]{:S(2)}, u32[]{:S(2)}) %collective-permute-start.1) | collective-permute-done | bytes 262176 | tf_op jit(solution)/shard_map/ppermute | solution.py:20
  37.9 20.9 %while.29 = (s32[]{:T(128)}, f32[4,64,2,4]{1,0,3,2:T(4,128)S(1)}, f32[4,64,2,4,128]{4,3,2,1,0:T(4,128)}, f32[4,64,2,4]{1,0,3,2:T(4,128)S(1)}, bf16[4,64,2,4,128]...) while((s32[]{:T(128)}, f32[4,64,2,4]{1,0,3,2:T(4,128)S(1)}, ...), condition=%wide.region_5.6_spmd, body=%wide.region_0.5_spmd.sunk | while | flops 68749824 | bytes 3850228 | solution.py:104
  38.1 4.1 %while.30 = (s32[]{:T(128)}, f32[64,2,4]{0,2,1:T(4,128)S(1)}, f32[64,2,4,128]{3,0,2,1:T(8,128)S(1)}, f32[64,2,4]{0,2,1:T(4,128)S(1)}, s32[]{:T(128)}, /*index=5*...) while((s32[]{:T(128)}, f32[64,2,4]{0,2,1:T(4,128)S(1)}, ...), condition=%wide.region_4.4_spmd, body=%wide.region_1.3_spmd.sunk | while | flops 68749824 | bytes 2526915 | solution.py:102
  42.2 0.9 copy_dynamic-update-slice_fusion.2
  43.3 4.1 %while.30 = (s32[]{:T(128)}, f32[64,2,4]{0,2,1:T(4,128)S(1)}, f32[64,2,4,128]{3,0,2,1:T(8,128)S(1)}, f32[64,2,4]{0,2,1:T(4,128)S(1)}, s32[]{:T(128)}, /*index=5*...) while((s32[]{:T(128)}, f32[64,2,4]{0,2,1:T(4,128)S(1)}, ...), condition=%wide.region_4.4_spmd, body=%wide.region_1.3_spmd.sunk | while | flops 68749824 | bytes 2526915 | solution.py:102
  47.5 0.9 copy_dynamic-update-slice_fusion.2
  48.5 4.1 %while.30 = (s32[]{:T(128)}, f32[64,2,4]{0,2,1:T(4,128)S(1)}, f32[64,2,4,128]{3,0,2,1:T(8,128)S(1)}, f32[64,2,4]{0,2,1:T(4,128)S(1)}, s32[]{:T(128)}, /*index=5*...) while((s32[]{:T(128)}, f32[64,2,4]{0,2,1:T(4,128)S(1)}, ...), condition=%wide.region_4.4_spmd, body=%wide.region_1.3_spmd.sunk | while | flops 68749824 | bytes 2526915 | solution.py:102
  52.7 0.9 copy_dynamic-update-slice_fusion.2
  53.8 4.1 %while.30 = (s32[]{:T(128)}, f32[64,2,4]{0,2,1:T(4,128)S(1)}, f32[64,2,4,128]{3,0,2,1:T(8,128)S(1)}, f32[64,2,4]{0,2,1:T(4,128)S(1)}, s32[]{:T(128)}, /*index=5*...) while((s32[]{:T(128)}, f32[64,2,4]{0,2,1:T(4,128)S(1)}, ...), condition=%wide.region_4.4_spmd, body=%wide.region_1.3_spmd.sunk | while | flops 68749824 | bytes 2526915 | solution.py:102
  57.9 0.9 copy_dynamic-update-slice_fusion.2
  59.3 8.4 %pmax.7 = bf16[256,8]{0,1:T(8,128)(2,1)S(1)} all-reduce(bf16[256,8]{0,1:T(8,128)(2,1)S(1)} %convert_element_type.27), channel_id=1, replica_groups=mesh['group'=2,'head'=4,'seq'=4] {'seq'}, use_global_device_ids=true, to_apply=%region_7.8 | all-reduce | flops 2048 | bytes 8192 | tf_op jit(solution)/shard_map/pmax | solution.py:134
  67.7 0.8 copy.54
  68.6 1.6 %reshape.147 = f32[256,1024]{1,0:T(8,128)S(1)} reshape(f32[4,64,2,4,128]{4,3,2,1,0:T(4,128)} %get-tuple-element.104) | data formatting | bytes 2097152 | tf_op jit(solution)/shard_map/reshape | solution.py:106
  70.4 1.6 %mul.75 = f32[256,2,4,128]{3,2,1,0:T(4,128)} broadcast(f32[256,2,4]{2,1,0:T(2,128)S(1)} %copy.39), dimensions={0,1,2} | broadcast | bytes 1056768 | tf_op jit(solution)/shard_map/mul | solution.py:139
  72.0 1.6 %mul.76 = f32[256,1024]{1,0:T(8,128)S(1)} reshape(f32[256,2,4,128]{3,2,1,0:T(4,128)} %mul.75) | data formatting | bytes 2097152 | tf_op jit(solution)/shard_map/mul | solution.py:139
  73.7 1.1 mul.77
  75.6 13.5 %all_gather.7 = bf16[256,256]{1,0:T(8,128)(2,1)S(1)} all-gather(bf16[64,256]{1,0:T(8,128)(2,1)S(1)} %copy-done.5), channel_id=1, replica_groups=mesh['group'=2,'head'=4,'seq'=4] {'seq'}, dimensions={0}, use_global_device_ids=true | all-gather | bytes 163840 | tf_op jit(solution)/shard_map/all_gather | solution.py:46
  90.2 0.8 copy.55
  91.1 24.3 %reduce-scatter.5.cloned.1.call-done = f32[64,1024]{1,0:T(8,128)} async-done(((f32[256,1024]{1,0:T(8,128)}), f32[64,1024]{1,0:T(8,128)}) %reduce-scatter.5.cloned.1.call-update) | async-done | bytes 262160 | tf_op jit(solution)/shard_map/reduce_scatter | solution.py:142
  115.5 0.8 copy-done.3
  (170 shorter events, 23.4 us)
Async XLA Ops:
  6.5 83.6 %reduce-scatter.7.cloned.1.call-start = ((), (), s32[]{:S(2)}) async-start(), calls=%async_computation.3 | async-start | bytes 163840
  6.5 20.6 %collective-permute-start = (bf16[64,1024]{1,0:T(8,128)(2,1)}, bf16[64,1024]{1,0:T(8,128)(2,1)S(1)}, u32[]{:S(2)}, u32[]{:S(2)}) collective-permute-start(bf16[64,1024]{1,0:T(8,128)(2,1)} %param.11), channel_id=1, source_target_pairs={{0,3},{1,0},{2,1},{3,2},{4,7},{5,4},{6,5},{7,6},{8,11},{9,8},{10,9... | collective-permute-start | bytes 393224 | tf_op jit(solution)/shard_map/ppermute | solution.py:20
  11.6 1.0 copy-start.4
  26.2 1.0 copy-start
  26.3 0.7 copy-start.6
  27.2 1.8 %copy-start.1 = (bf16[1024,256]{1,0:T(8,128)(2,1)S(1)}, bf16[1024,256]{1,0:T(8,128)(2,1)}, u32[]{:S(2)}) copy-start(bf16[1024,256]{1,0:T(8,128)(2,1)} %param.14) | copy-start | bytes 1572868
  27.2 10.2 %collective-permute-start.1 = (bf16[128,1024]{1,0:T(8,128)(2,1)S(1)}, bf16[128,1024]{1,0:T(8,128)(2,1)S(1)}, u32[]{:S(2)}, u32[]{:S(2)}) collective-permute-start(bf16[128,1024]{1,0:T(8,128)(2,1)S(1)} %pad_maximum_fusion), channel_id=1, source_target_pairs={{0,2},{1,3},{2,0},{3,1},{4,6},{5,7},{6,4},{7,5},{8,10},{9,11},{10,... | collective-permute-start | bytes 786440 | tf_op jit(solution)/shard_map/ppermute | solution.py:20
  29.2 1.0 copy-start.2
  68.6 46.8 %reduce-scatter.5.cloned.1.call-start = ((), (), s32[]{:S(2)}) async-start(), calls=%async_computation.2 | async-start | bytes 1310720 | tf_op jit(solution)/shard_map/reduce_scatter | solution.py:142
  74.8 0.8 copy-start.5
  115.3 0.9 copy-start.3
Sparse Core Ops, SparseCore 0:
  68.7 18.7 reduce-scatter.6
  89.9 25.3 reduce-scatter.4
